TPU v7x, 256 devices: a whole 4x4x8 slice. The times are simulated.
256 devices in a mesh: space: 16 (over x, y), mode: 16 (over z, core).
Axes of the slice: x: 4, y: 4, z: 8, core: 2. Of those that a mesh axis runs over, the one named last changes fastest.
Arguments:
- density: float32 [512, 32, 256], P('mode', 'space'), may hold values from -6 to 6
- tensor: bfloat16 [512, 512, 512], P('mode', 'space'), may hold values from -0.01171875 to 0.01171875
- velocity: float32 [3, 512], P(None, 'mode'), may hold values from -1 to 1
- inflow: float32 [512], P('mode'), may hold values from -6 to 6
- flags: int32 [2, 256], replicated, may hold values 0 or 1
Outputs:
- collided: float32 [512, 32, 256], P('mode', 'space')
All inputs are finite; a program needn't handle non-finite values.
Results may differ from a plain program's by a relative error of at most 0.0025.
Values may be sent and summed in bfloat16 or wider, within the bound.
No kernel may reach another device: no remote copies, remote signals or barrier semaphores. Data moves between devices by JAX's collectives and lax.ppermute only.
A program may use at most 128 MiB of HBM per device.

v0:
```python
import jax
import jax.numpy as jnp
from jax import lax
from jax.sharding import PartitionSpec as P

NXY = 16
SUBSTEPS = 3


courant = 0.3
time_step = 0.5


def with_halo(block, sides, width):
    for axis, dim in sides:
        count = lax.axis_size(axis)
        forward = [(i, i + 1) for i in range(count - 1)]
        backward = [(target, source) for source, target in forward]
        low = lax.ppermute(
            lax.slice_in_dim(block, block.shape[dim] - width, None, axis=dim), axis, forward
        )
        high = lax.ppermute(lax.slice_in_dim(block, 0, width, axis=dim), axis, backward)
        block = jnp.concatenate([low, block, high], axis=dim)
    return block


def neighbours(field):
    rows, planes, cells = field.shape
    grid = field.reshape(rows, planes, NXY, NXY)
    padded = jnp.pad(grid, ((0, 0), (0, 0), (1, 1), (1, 1)))
    lower_x = padded[:, :, :-2, 1:-1].reshape(field.shape)
    upper_x = padded[:, :, 2:, 1:-1].reshape(field.shape)
    lower_y = padded[:, :, 1:-1, :-2].reshape(field.shape)
    upper_y = padded[:, :, 1:-1, 2:].reshape(field.shape)
    return (lower_x, upper_x, lower_y, upper_y)


def upwind(field, below, above, velocity):
    lower_x, upper_x, lower_y, upper_y = neighbours(field)
    lowers = [lower_x, lower_y, below]
    uppers = [upper_x, upper_y, above]
    flux = jnp.zeros_like(field)
    for direction in range(3):
        speed = velocity[direction][:, None, None]
        flux = flux + jnp.maximum(speed, 0.0) * (field - lowers[direction])
        flux = flux + jnp.minimum(speed, 0.0) * (uppers[direction] - field)
    return field - courant * flux


def per_device(density, tensor, velocity, inflow, flags):
    position = lax.axis_index("space")
    final = lax.axis_size("space") - 1
    ghost_low = flags[0].astype(jnp.float32)[None, :] * inflow[:, None]
    ghost_high = flags[1].astype(jnp.float32)[None, :] * inflow[:, None]
    field = density
    for substep in range(SUBSTEPS):
        padded = with_halo(field, (("space", 1),), 1)
        low_plane = jnp.where(position == 0, ghost_low, padded[:, 0])
        high_plane = jnp.where(position == final, ghost_high, padded[:, -1])
        below = jnp.concatenate([low_plane[:, None], padded[:, 1:-2]], axis=1)
        above = jnp.concatenate([padded[:, 2:-1], high_plane[:, None]], axis=1)
        field = upwind(field, below, above, velocity)
    coarse = field.astype(jnp.bfloat16)
    full_modes = lax.all_gather(coarse, "mode", axis=0, tiled=True)
    out_rows, pair_rows, width = tensor.shape
    columns = full_modes.reshape(width, -1)
    piece = lax.all_gather(tensor, "space", axis=1, tiled=True)
    count = piece.shape[1]
    inner = jnp.dot(
        piece.reshape(out_rows * count, width), columns, preferred_element_type=jnp.float32
    )
    factor = columns.astype(jnp.float32)
    gain = jnp.sum(inner.reshape(out_rows, count, -1) * factor[None], axis=1).reshape(field.shape)
    return field + time_step * gain


def solution(mesh):
    in_specs = (P("mode", "space", None), P("mode", "space", None), P(None, "mode"), P("mode"), P())
    out_specs = P("mode", "space", None)
    return jax.shard_map(
        per_device, mesh=mesh, in_specs=in_specs, out_specs=out_specs, check_vma=False
    )
```

profile of v0, /device:TPU:1, one launch (start us, length us, event | category | flops | bytes accessed | tf_op | source)
XLA Modules:
  0.0 196.7 jit_solution(18217028310613476053)
XLA Ops:
  6.5 0.7 all-gather.2.cloned.1.call-update
  7.3 1.0 fusion.22
  8.2 1.3 collective-permute-start.1
  9.6 4.6 %collective-permute-start = (f32[32,1,256]{2,0,1:T(8,128)S(1)}, f32[32,1,256]{2,0,1:T(8,128)S(1)}, u32[]{:S(2)}, u32[]{:S(2)}) collective-permute-start(f32[32,1,256]{2,0,1:T(8,128)S(1)} %copy.152), channel_id=1, source_target_pairs={{0,16},{16,32},{32,48},{48,64},{64,80},{80,96},{96,112},{112,128},... | collective-permute-start | bytes 98312 | tf_op jit(solution)/shard_map/ppermute | solution.py:19
  14.2 1.0 copy.117
  15.2 0.8 slice_convert_fusion
  16.0 0.8 maximum_bitcast_fusion.2
  16.9 0.1 copy.123
  17.0 0.1 copy.120
  17.2 0.1 copy.119
  17.3 0.7 multiply_select_fusion.2
  18.0 1.0 fusion.4
  19.0 0.1 copy.131
  19.1 1.3 collective-permute-start.3
  20.4 4.0 %collective-permute-start.2 = (f32[32,1,256]{2,0,1:T(8,128)S(1)}, f32[32,1,256]{2,0,1:T(8,128)S(1)}, u32[]{:S(2)}, u32[]{:S(2)}) collective-permute-start(f32[32,1,256]{2,0,1:T(8,128)S(1)} %get-tuple-element.21), channel_id=1, source_target_pairs={{0,16},{16,32},{32,48},{48,64},{64,80},{80,96},{96,112},{112,128},... | collective-permute-start | bytes 98312 | tf_op jit(solution)/shard_map/ppermute | solution.py:19
  24.5 0.1 copy.135
  24.7 0.1 copy.133
  24.9 0.5 collective-permute-done.2
  25.4 0.7 multiply_select_fusion.1
  26.3 0.1 copy.136
  26.4 3.6 %collective-permute-start.4 = (f32[32,1,256]{2,0,1:T(8,128)S(1)}, f32[32,1,256]{2,0,1:T(8,128)S(1)}, u32[]{:S(2)}, u32[]{:S(2)}) collective-permute-start(f32[32,1,256]{2,0,1:T(8,128)S(1)} %get-tuple-element.19), channel_id=1, source_target_pairs={{0,16},{16,32},{32,48},{48,64},{64,80},{80,96},{96,112},{112,128},... | collective-permute-start | bytes 98312 | tf_op jit(solution)/shard_map/ppermute | solution.py:19
  30.1 1.3 collective-permute-start.5
  31.9 5.3 %collective-permute-done.5 = f32[32,1,256]{2,0,1:T(8,128)S(1)} collective-permute-done((f32[32,1,256]{2,0,1:T(8,128)S(1)}, f32[32,1,256]{2,0,1:T(8,128)S(1)}, u32[]{:S(2)}, u32[]{:S(2)}) %collective-permute-start.5) | collective-permute-done | bytes 32800 | tf_op jit(solution)/shard_map/ppermute | solution.py:22
  37.2 0.7 multiply_select_fusion.3
  37.9 0.1 fusion.18
  38.1 24.7 %all_gather.6 = bf16[512,2,256]{2,1,0:T(2,128)(2,1)S(1)} all-gather(bf16[32,2,256]{2,1,0:T(2,128)(2,1)S(1)} %copy.141), channel_id=1, replica_groups=mesh['space'=16,'mode'=16] {'mode'}, dimensions={0}, use_global_device_ids=true | all-gather | bytes 557056 | tf_op jit(solution)/shard_map/all_gather | solution.py:64
  62.9 0.2 copy.142
  63.1 67.3 %all-gather.2.cloned.1.call-done = bf16[32,512,512]{2,1,0:T(8,128)(2,1)} async-done(((bf16[32,32,512]{2,1,0:T(8,128)(2,1)}), bf16[32,512,512]{2,1,0:T(8,128)(2,1)}) %all-gather.2.cloned.1.call-update) | async-done | bytes 16777232 | tf_op jit(solution)/shard_map/all_gather | solution.py:67
  130.4 23.2 %fusion.23 = f32[512,16384]{1,0:T(8,128)} fusion(bf16[512,512]{1,0:T(8,128)(2,1)S(1)} %bitcast.44, bf16[16384,512]{1,0:T(8,128)(2,1)} %bitcast.42), kind=kOutput, calls=%fused_computation.56 | convolution fusion | flops 8589934592 | bytes 50855936 | tf_op jit(solution)/shard_map/dot_general | solution.py:69
  153.6 32.5 %copy.149 = f32[64,8,32,512]{3,2,1,0:T(8,128)S(1)} copy(f32[64,8,32,512]{3,1,2,0:T(8,128)} %bitcast.40) | data formatting | bytes 67108864
  186.1 3.0 %multiply_reduce_fusion = f32[32,512]{0,1:T(8,128)S(1)} fusion(f32[32,512,512]{1,0,2:T(8,128)S(1)} %bitcast.41, f32[512,512]{0,1:T(8,128)S(1)} %copy.142), kind=kLoop, calls=%fused_computation | loop fusion | flops 16760832 | bytes 34668544 | tf_op jit(solution)/shard_map/reduce_sum | solution.py:73
  189.2 0.7 copy.145
  (25 shorter events, 1.4 us)
Async XLA Ops:
  6.5 123.9 %all-gather.2.cloned.1.call-start = ((), (), s32[]{:S(2)}) async-start(), calls=%async_computation | async-start | bytes 17825792 | tf_op jit(solution)/shard_map/all_gather | solution.py:67
  8.2 9.0 %collective-permute-start.1 = (f32[32,1,256]{2,0,1:T(8,128)S(1)}, f32[32,1,256]{2,0,1:T(8,128)S(1)}, u32[]{:S(2)}, u32[]{:S(2)}) collective-permute-start(f32[32,1,256]{2,0,1:T(8,128)S(1)} %copy.151), channel_id=1, source_target_pairs={{16,0},{32,16},{48,32},{64,48},{80,64},{96,80},{112,96},{128,112},... | collective-permute-start | bytes 98312 | tf_op jit(solution)/shard_map/ppermute | solution.py:22
  9.6 7.7 %collective-permute-start = (f32[32,1,256]{2,0,1:T(8,128)S(1)}, f32[32,1,256]{2,0,1:T(8,128)S(1)}, u32[]{:S(2)}, u32[]{:S(2)}) collective-permute-start(f32[32,1,256]{2,0,1:T(8,128)S(1)} %copy.152), channel_id=1, source_target_pairs={{0,16},{16,32},{32,48},{48,64},{64,80},{80,96},{96,112},{112,128},... | collective-permute-start | bytes 98312 | tf_op jit(solution)/shard_map/ppermute | solution.py:19
  19.1 5.8 %collective-permute-start.3 = (f32[32,1,256]{2,0,1:T(8,128)S(1)}, f32[32,1,256]{2,0,1:T(8,128)S(1)}, u32[]{:S(2)}, u32[]{:S(2)}) collective-permute-start(f32[32,1,256]{2,0,1:T(8,128)S(1)} %get-tuple-element.22), channel_id=1, source_target_pairs={{16,0},{32,16},{48,32},{64,48},{80,64},{96,80},{112,96},{128,112},... | collective-permute-start | bytes 98312 | tf_op jit(solution)/shard_map/ppermute | solution.py:22
  20.4 5.0 %collective-permute-start.2 = (f32[32,1,256]{2,0,1:T(8,128)S(1)}, f32[32,1,256]{2,0,1:T(8,128)S(1)}, u32[]{:S(2)}, u32[]{:S(2)}) collective-permute-start(f32[32,1,256]{2,0,1:T(8,128)S(1)} %get-tuple-element.21), channel_id=1, source_target_pairs={{0,16},{16,32},{32,48},{48,64},{64,80},{80,96},{96,112},{112,128},... | collective-permute-start | bytes 98312 | tf_op jit(solution)/shard_map/ppermute | solution.py:19
  26.4 5.5 %collective-permute-start.4 = (f32[32,1,256]{2,0,1:T(8,128)S(1)}, f32[32,1,256]{2,0,1:T(8,128)S(1)}, u32[]{:S(2)}, u32[]{:S(2)}) collective-permute-start(f32[32,1,256]{2,0,1:T(8,128)S(1)} %get-tuple-element.19), channel_id=1, source_target_pairs={{0,16},{16,32},{32,48},{48,64},{64,80},{80,96},{96,112},{112,128},... | collective-permute-start | bytes 98312 | tf_op jit(solution)/shard_map/ppermute | solution.py:19
  30.1 7.1 %collective-permute-start.5 = (f32[32,1,256]{2,0,1:T(8,128)S(1)}, f32[32,1,256]{2,0,1:T(8,128)S(1)}, u32[]{:S(2)}, u32[]{:S(2)}) collective-permute-start(f32[32,1,256]{2,0,1:T(8,128)S(1)} %get-tuple-element.20), channel_id=1, source_target_pairs={{16,0},{32,16},{48,32},{64,48},{80,64},{96,80},{112,96},{128,112},... | collective-permute-start | bytes 98312 | tf_op jit(solution)/shard_map/ppermute | solution.py:22
Sparse Core Ops, SparseCore 0:
  9.8 120.5 all-gather.1
where the time goes:
time: 197 us
  waiting for transfers between devices  73.8 us (37%)
  local copies, waits for them, and re-layouts  37.3 us (19%)
  blocking collectives  24.7 us (13%)
  matrix products  23.2 us (12%)
  starting transfers between devices  16.2 us (8%)
  between operations  13.6 us (7%)
  other arithmetic  7.92 us (4%)
    all_gather x1, waiting for transfers between devices, per_device(): piece = lax.all_gather(tensor, 'space', axis=1, tiled=True)  67.3 us
    unnamed x5, local copies, waits for them, and re-layouts  33.6 us
    all_gather x1, blocking collectives, per_device(): full_modes = lax.all_gather(coarse, 'mode', axis=0, tiled=True)  24.7 us
    dot_general x1, matrix products, per_device(): jnp.dot(piece.reshape(out_rows * count, width), columns, preferred_elemen...  23.2 us
    ppermute x3, starting transfers between devices, with_halo(): lax.ppermute(lax.slice_in_dim(block, block.shape[dim] - width, None, axis...  12.3 us
    ppermute x3, waiting for transfers between devices, with_halo(): lax.ppermute(lax.slice_in_dim(block, 0, width, axis=dim), axis, backward)  5.28 us
  transfers between devices with their start and end apart: 7, of which 3 were waited for; matrix products, arithmetic and copies ran while one was open for 5% of the time, Pallas kernels for 0%

commit v1 on v0

v1 whole, which is shorter than its diff:
```python
import functools

import jax
import jax.numpy as jnp
from jax import lax
from jax.experimental import pallas as pl
from jax.experimental.pallas import tpu as pltpu
from jax.sharding import Mesh
from jax.sharding import PartitionSpec as P

NXY = 16
SUBSTEPS = 3
HALO = SUBSTEPS

courant = 0.3
time_step = 0.5

SPACE = ("sx", "sy")
MODE = ("mz", "mc")


def neighbours(field):
    rows, planes, cells = field.shape
    grid = field.reshape(rows, planes, NXY, NXY)
    padded = jnp.pad(grid, ((0, 0), (0, 0), (1, 1), (1, 1)))
    lower_x = padded[:, :, :-2, 1:-1].reshape(field.shape)
    upper_x = padded[:, :, 2:, 1:-1].reshape(field.shape)
    lower_y = padded[:, :, 1:-1, :-2].reshape(field.shape)
    upper_y = padded[:, :, 1:-1, 2:].reshape(field.shape)
    return (lower_x, upper_x, lower_y, upper_y)


def upwind(field, below, above, velocity):
    lower_x, upper_x, lower_y, upper_y = neighbours(field)
    lowers = [lower_x, lower_y, below]
    uppers = [upper_x, upper_y, above]
    flux = jnp.zeros_like(field)
    for direction in range(3):
        speed = velocity[direction][:, None, None]
        flux = flux + jnp.maximum(speed, 0.0) * (field - lowers[direction])
        flux = flux + jnp.minimum(speed, 0.0) * (uppers[direction] - field)
    return field - courant * flux


def shifted(block, count, distance, planes):
    if distance > 0:
        pairs = [(i, i + distance) for i in range(count - distance)]
        piece = block[:, block.shape[1] - planes :]
    else:
        pairs = [(i, i + distance) for i in range(-distance, count)]
        piece = block[:, :planes]
    return lax.ppermute(piece, SPACE, pairs)


def transport(density, velocity, ghost_low, ghost_high):
    count = lax.axis_size(SPACE)
    position = lax.axis_index(SPACE)
    depth = density.shape[1]
    total_planes = count * depth
    below, above = [], []
    need = HALO
    distance = 1
    while need > 0:
        take = min(need, depth)
        below.insert(0, shifted(density, count, distance, take))
        above.append(shifted(density, count, -distance, take))
        need -= take
        distance += 1
    ext = jnp.concatenate(below + [density] + above, axis=1)
    planes = ext.shape[1]
    z = position * depth - HALO + lax.broadcasted_iota(jnp.int32, (1, planes, 1), 1)
    low_mask = z < 0
    high_mask = z >= total_planes

    def fix(f):
        f = jnp.where(low_mask, ghost_low[:, None, :], f)
        return jnp.where(high_mask, ghost_high[:, None, :], f)

    field = fix(ext)
    for _ in range(SUBSTEPS):
        lower = jnp.concatenate([field[:, :1], field[:, :-1]], axis=1)
        upper = jnp.concatenate([field[:, 1:], field[:, -1:]], axis=1)
        field = fix(upwind(field, lower, upper, velocity))
    return field[:, HALO : HALO + depth]


def gain_kernel(t_ref, x_ref, xi_ref, o_ref, *, group, rows):
    x = x_ref[...]
    xi = xi_ref[...].astype(jnp.float32)
    n_groups = o_ref.shape[0] // group

    def body(g, carry):
        start = pl.multiple_of(g * group * rows, group * rows)
        t = t_ref[pl.ds(start, group * rows), :]
        inner = jnp.dot(t, x, preferred_element_type=jnp.float32)
        inner = inner.reshape(group, rows, inner.shape[-1])
        o_ref[pl.ds(pl.multiple_of(g * group, group), group), :] = jnp.sum(
            inner * xi[None], axis=1
        )
        return carry

    lax.fori_loop(0, n_groups, body, 0)


def contract(tensor2d, columns, factor, k_count, tile=512, group=8):
    kr, width = tensor2d.shape
    rows = kr // k_count
    cells = columns.shape[1]
    kernel = functools.partial(gain_kernel, group=group, rows=rows)
    return pl.pallas_call(
        kernel,
        out_shape=jax.ShapeDtypeStruct((k_count, cells), jnp.float32),
        grid=(cells // tile,),
        in_specs=[
            pl.BlockSpec((kr, width), lambda c: (0, 0)),
            pl.BlockSpec((width, tile), lambda c: (0, c)),
            pl.BlockSpec((rows, tile), lambda c: (0, c)),
        ],
        out_specs=pl.BlockSpec((k_count, tile), lambda c: (0, c)),
        compiler_params=pltpu.CompilerParams(vmem_limit_bytes=48 * 1024 * 1024),
        cost_estimate=pl.CostEstimate(
            flops=2 * kr * width * cells + 2 * kr * cells,
            bytes_accessed=kr * width * 2 + width * cells * 2 + rows * cells * 2 + k_count * cells * 4,
            transcendentals=0,
        ),
    )(tensor2d, columns, factor)


def per_device(density, tensor, velocity, inflow, flags):
    rows, depth, cells = density.shape
    ghost_low = flags[0].astype(jnp.float32)[None, :] * inflow[:, None]
    ghost_high = flags[1].astype(jnp.float32)[None, :] * inflow[:, None]

    pair_tensor = lax.all_gather(tensor, "mc", axis=0, tiled=True)

    field = transport(density, velocity, ghost_low, ghost_high)

    coarse = field.astype(jnp.bfloat16)
    mine = lax.all_to_all(coarse, "mc", 1, 0, tiled=True)
    mine = lax.all_gather(mine, "mz", axis=0, tiled=True)
    modes = mine.shape[0]
    columns = lax.all_gather(mine.reshape(modes, cells), SPACE, axis=1, tiled=True)

    k_count, i_count, width = pair_tensor.shape
    position = lax.axis_index(SPACE)
    factor = lax.dynamic_slice_in_dim(columns, position * i_count, i_count, axis=0)
    partial = contract(pair_tensor.reshape(k_count * i_count, width), columns, factor, k_count)

    count = lax.axis_size(SPACE)
    partial = partial.reshape(k_count, count, cells)
    gain = lax.psum_scatter(partial, SPACE, scatter_dimension=1, tiled=True)
    gain = lax.all_to_all(gain, "mc", 0, 1, tiled=True)
    return field + time_step * gain.reshape(field.shape)


def solution(mesh):
    devices = mesh.devices
    space, mode = devices.shape
    fine = Mesh(devices.reshape(4, space // 4, mode // 2, 2), SPACE + MODE)
    in_specs = (P(MODE, SPACE, None), P(MODE, SPACE, None), P(None, MODE), P(MODE), P())
    out_specs = P(MODE, SPACE, None)
    return jax.shard_map(
        per_device, mesh=fine, in_specs=in_specs, out_specs=out_specs, check_vma=False
    )
```

time: 197 us -> 300 us (1.52)
  waiting for transfers between devices: 73.8 us -> 164 us
  matrix products: 23.2 us -> 0 us
  Pallas kernels: 0 us -> 22 us
  blocking collectives: 24.7 us -> 34.8 us
  other arithmetic: 7.92 us -> 13.8 us
  starting transfers between devices: 16.2 us -> 12.3 us
    unnamed x1 -> x4, waiting for transfers between devices: 0.71 us -> 78.8 us
    unnamed x5 -> x92, local copies, waits for them, and re-layouts: 33.6 us -> 6.04 us
    dot_general x1 -> x0, matrix products: 23.2 us -> none  [per_device(): jnp.dot(piece.reshape(out_rows * count, width), columns, preferred_elemen...]
    pallas_call x0 -> x1, Pallas kernels: none -> 22 us  [contract(): pl.pallas_call(kernel, out_shape=jax.ShapeDtypeStruct((k_count, cells), j...]
    all_gather x1 -> x2, waiting for transfers between devices: 67.3 us -> 84.7 us  [the longest x1 66.5 us: per_device(): lax.all_gather(mine.reshape(modes, cells), SPACE, axis=1, tiled=True)]
    all_to_all x0 -> x2, blocking collectives: none -> 10.7 us  [the longest x1 5.79 us: per_device(): gain = lax.all_to_all(gain, 'mc', 0, 1, tiled=True)]
    slice x3 -> x19, local copies, waits for them, and re-layouts: 0.99 us -> 11 us  [the longest x8 4.09 us: transport(): upper = jnp.concatenate([field[:, 1:], field[:, -1:]], axis=1)]
    ppermute x6 -> x4, waiting for transfers between devices: 5.77 us -> 0.01 us  [shifted(): return lax.ppermute(piece, SPACE, pairs)]
  transfers between devices with their start and end apart: 7 -> 7, of which waited for: 3 -> 3; matrix products, arithmetic and copies ran while one was open for 5% -> 3% of each run, Pallas kernels for 0% -> 0%
where the time goes in v1:
time: 300 us; the launch traced here: 299 us
  waiting for transfers between devices  164 us (55%)
  local copies, waits for them, and re-layouts  39 us (13%)
  blocking collectives  34.8 us (12%)
  Pallas kernels  22 us (7%)
  other arithmetic  13.8 us (5%)
  between operations  13.8 us (5%)
  starting transfers between devices  12.3 us (4%)
    unnamed x4, waiting for transfers between devices  78.8 us
    all_gather x1, waiting for transfers between devices, per_device(): lax.all_gather(mine.reshape(modes, cells), SPACE, axis=1, tiled=True)  66.5 us
    all_gather x1, blocking collectives, per_device(): mine = lax.all_gather(mine, 'mz', axis=0, tiled=True)  24.1 us
    pallas_call x1, Pallas kernels, contract(): pl.pallas_call(kernel, out_shape=jax.ShapeDtypeStruct((k_count, cells), j...  22 us
    all_gather x1, waiting for transfers between devices, per_device(): pair_tensor = lax.all_gather(tensor, 'mc', axis=0, tiled=True)  18.3 us
    ppermute x4, starting transfers between devices, shifted(): return lax.ppermute(piece, SPACE, pairs)  12.2 us
    unnamed x92, local copies, waits for them, and re-layouts  6.04 us
  transfers between devices with their start and end apart: 7, of which 3 were waited for; matrix products, arithmetic and copies ran while one was open for 3% of the time, Pallas kernels for 0%

profile of v1, /device:TPU:1, one launch (start us, length us, event | category | flops | bytes accessed | tf_op | source)
XLA Modules:
  0.0 299.2 jit_solution(12130026072394681167)
XLA Ops:
  7.5 4.0 %collective-permute-start.1 = (f32[32,2,256]{2,0,1:T(8,128)S(1)}, f32[32,2,256]{2,0,1:T(8,128)S(1)}, u32[]{:S(2)}, u32[]{:S(2)}) collective-permute-start(f32[32,2,256]{2,0,1:T(8,128)S(1)} %copy.69), channel_id=1, source_target_pairs={{0,16},{16,32},{32,48},{48,64},{64,80},{80,96},{96,112},{112,128},... | collective-permute-start | bytes 196616 | tf_op jit(solution)/shard_map/ppermute | solution.py:52
  11.5 1.3 collective-permute-start.2
  12.8 5.6 %collective-permute-start = (f32[32,1,256]{2,0,1:T(8,128)S(1)}, f32[32,1,256]{2,0,1:T(8,128)S(1)}, u32[]{:S(2)}, u32[]{:S(2)}) collective-permute-start(f32[32,1,256]{2,0,1:T(8,128)S(1)} %get-tuple-element.38), channel_id=1, source_target_pairs={{0,32},{16,48},{32,64},{48,80},{64,96},{80,112},{96,128},{112,144}... | collective-permute-start | bytes 98312 | tf_op jit(solution)/shard_map/ppermute | solution.py:52
  18.4 1.3 collective-permute-start.3
  21.4 1.4 maximum_bitcast_fusion.2
  27.9 1.2 copy.84
  29.2 1.3 copy.85
  31.9 1.1 pad_slice_fusion.10
  33.5 2.2 pad_slice_fusion.11
  35.7 2.3 copy.79
  38.9 1.0 copy.82
  40.5 1.8 fusion.22
  42.4 1.2 copy.92
  43.6 1.2 copy.93
  46.4 1.1 pad_slice_fusion.6
  48.0 3.2 %pad_slice_fusion.7 = (f32[32,8,16,16]{0,3,2,1:T(8,128)}, f32[32,8,16,16]{0,3,2,1:T(8,128)S(1)}, f32[32,8,16,16]{0,3,2,1:T(8,128)S(1)}, f32[32,8,16,16]{0,3,2,1:T(8,128)S(1)}) fusion(f32[32,8,16,16]{0,3,2,1:T(8,128)S(1)} %get-tuple-element.21, f32[32,1,16,16]{0,3,2,1:T(8,128)S(1)} %bitcast.83, f32[32,7,16,16]{0,3,2,1:T(8,128)S(1)} %bitcast.76, ...), kind=kLoop, calls=%fused_computation.7 | loop fusion | flops 1507328 | bytes 1901328 | tf_op jit(solution)/shard_map/slice | solution.py:26
  51.2 1.9 pad_slice_fusion.3
  54.0 2.3 copy.96
  56.4 2.3 copy.97
  58.6 2.2 copy.98
  60.9 1.0 copy.87
  61.9 1.0 copy.89
  64.4 1.7 multiply_add_fusion
  66.9 4.9 %all_to_all.27 = bf16[32,2,256]{2,0,1:T(8,128)(2,1)S(1)} all-to-all(bf16[32,2,256]{2,0,1:T(8,128)(2,1)S(1)} %get-tuple-element.7), channel_id=1, replica_groups=mesh['sx'=4,'sy'=4,'mz'=8,'mc'=2] {'mc'}, dimensions={1} | all-to-all | bytes 65536 | tf_op jit(solution)/shard_map/all_to_all | solution.py:139
  71.8 24.1 %all_gather.10 = bf16[512,1,256]{2,0,1:T(8,128)(2,1)} all-gather(bf16[64,1,256]{2,0,1:T(8,128)(2,1)S(1)} %bitcast.87), channel_id=1, replica_groups=mesh['sx'=4,'sy'=4,'mz'=8,'mc'=2] {'mz'}, dimensions={0}, use_global_device_ids=true | all-gather | bytes 294912 | tf_op jit(solution)/shard_map/all_gather | solution.py:140
  96.7 66.5 %all-gather.6.cloned.1.call-done = bf16[512,1,4096]{2,0,1:T(8,128)(2,1)} async-done(((bf16[512,1,256]{2,0,1:T(8,128)(2,1)}), bf16[512,1,4096]{2,0,1:T(8,128)(2,1)}) %all-gather.6.cloned.1.call-update) | async-done | bytes 4194320 | tf_op jit(solution)/shard_map/all_gather | solution.py:142
  164.1 18.3 %all-gather.4.cloned.1.call-done = bf16[64,32,512]{2,1,0:T(8,128)(2,1)} async-done(((bf16[32,32,512]{2,1,0:T(8,128)(2,1)}), bf16[64,32,512]{2,1,0:T(8,128)(2,1)}) %all-gather.4.cloned.1.call-update) | async-done | bytes 2097168 | tf_op jit(solution)/shard_map/all_gather | solution.py:134
  182.4 1.6 copy-done
  184.0 22.0 %shard_map.55 = f32[64,4096]{1,0:T(8,128)S(1)} custom-call(bf16[2048,512]{1,0:T(8,128)(2,1)S(1)} %bitcast.59, bf16[512,4096]{1,0:T(8,128)(2,1)} %bitcast.88, bf16[32,4096]{1,0:T(8,128)(2,1)S(1)} %dynamic-slice_bitcast_fusion.xi_ref), custom_call_target="tpu_custom_call" | custom-call | flops 8606711808 | bytes 7602176 | tf_op jit(solution)/shard_map/pallas_call | solution.py:110
  206.1 1.1 copy.107
  207.2 78.0 %reduce-scatter.4.cloned.1.call-done = f32[64,1,256]{2,0,1:T(8,128)} async-done(((f32[64,16,256]{2,0,1:T(8,128)}), f32[64,1,256]{2,0,1:T(8,128)}) %reduce-scatter.4.cloned.1.call-update) | async-done | bytes 65552
  286.2 5.8 %all_to_all.28 = f32[64,1,256]{2,1,0:T(1,128)S(1)} all-to-all(f32[64,1,256]{2,1,0:T(1,128)S(1)} %copy.100), channel_id=1, replica_groups=mesh['sx'=4,'sy'=4,'mz'=8,'mc'=2] {'mc'}, dimensions={0} | all-to-all | bytes 131072 | tf_op jit(solution)/shard_map/all_to_all | solution.py:152
  (141 shorter events, 19.4 us)
Async XLA Ops:
  6.5 20.4 %copy-start.21 = (f32[32,2,256]{2,1,0:T(2,128)S(1)}, f32[32,2,256]{2,1,0:T(2,128)}, u32[]{:S(2)}) copy-start(f32[32,2,256]{2,1,0:T(2,128)} %param.5) | copy-start | bytes 196612
  6.5 156.6 %all-gather.6.cloned.1.call-start = ((), (), s32[]{:S(2)}) async-start(), calls=%async_computation.4 | async-start | bytes 4456448 | tf_op jit(solution)/shard_map/all_gather | solution.py:142
  7.5 19.5 %collective-permute-start.1 = (f32[32,2,256]{2,0,1:T(8,128)S(1)}, f32[32,2,256]{2,0,1:T(8,128)S(1)}, u32[]{:S(2)}, u32[]{:S(2)}) collective-permute-start(f32[32,2,256]{2,0,1:T(8,128)S(1)} %copy.69), channel_id=1, source_target_pairs={{0,16},{16,32},{32,48},{48,64},{64,80},{80,96},{96,112},{112,128},... | collective-permute-start | bytes 196616 | tf_op jit(solution)/shard_map/ppermute | solution.py:52
  11.5 15.5 %collective-permute-start.2 = (f32[32,2,256]{2,0,1:T(8,128)S(1)}, f32[32,2,256]{2,0,1:T(8,128)S(1)}, u32[]{:S(2)}, u32[]{:S(2)}) collective-permute-start(f32[32,2,256]{2,0,1:T(8,128)S(1)} %copy.69), channel_id=1, source_target_pairs={{16,0},{32,16},{48,32},{64,48},{80,64},{96,80},{112,96},{128,112},... | collective-permute-start | bytes 196616 | tf_op jit(solution)/shard_map/ppermute | solution.py:52
  12.8 13.9 %collective-permute-start = (f32[32,1,256]{2,0,1:T(8,128)S(1)}, f32[32,1,256]{2,0,1:T(8,128)S(1)}, u32[]{:S(2)}, u32[]{:S(2)}) collective-permute-start(f32[32,1,256]{2,0,1:T(8,128)S(1)} %get-tuple-element.38), channel_id=1, source_target_pairs={{0,32},{16,48},{32,64},{48,80},{64,96},{80,112},{96,128},{112,144}... | collective-permute-start | bytes 98312 | tf_op jit(solution)/shard_map/ppermute | solution.py:52
  18.4 8.4 %collective-permute-start.3 = (f32[32,1,256]{2,0,1:T(8,128)S(1)}, f32[32,1,256]{2,0,1:T(8,128)S(1)}, u32[]{:S(2)}, u32[]{:S(2)}) collective-permute-start(f32[32,1,256]{2,0,1:T(8,128)S(1)} %get-tuple-element.37), channel_id=1, source_target_pairs={{32,0},{48,16},{64,32},{80,48},{96,64},{112,80},{128,96},{144,112}... | collective-permute-start | bytes 98312 | tf_op jit(solution)/shard_map/ppermute | solution.py:52
  23.5 5.7 %copy-start.17 = (f32[32,256]{1,0:T(8,128)}, f32[32,256]{1,0:T(8,128)S(1)}, u32[]{:S(2)}) copy-start(f32[32,256]{1,0:T(8,128)S(1)} %get-tuple-element.47) | copy-start | bytes 98308
  23.5 5.7 %copy-start.19 = (f32[32,256]{1,0:T(8,128)}, f32[32,256]{1,0:T(8,128)S(1)}, u32[]{:S(2)}) copy-start(f32[32,256]{1,0:T(8,128)S(1)} %get-tuple-element.48) | copy-start | bytes 98308
  24.4 8.7 %copy-start.7 = (f32[32,16,16]{0,2,1:T(8,128)}, f32[32,16,16]{0,2,1:T(8,128)S(1)}, u32[]{:S(2)}) copy-start(f32[32,16,16]{0,2,1:T(8,128)S(1)} %get-tuple-element.50) | copy-start | bytes 98308
  27.9 3.6 %copy-start.8 = (f32[32,7,256]{2,0,1:T(8,128)}, f32[32,7,256]{2,0,1:T(8,128)S(1)}, u32[]{:S(2)}) copy-start(f32[32,7,256]{2,0,1:T(8,128)S(1)} %get-tuple-element.33) | copy-start | bytes 688132
  27.9 3.6 %copy-start.9 = (f32[32,7,256]{2,0,1:T(8,128)}, f32[32,7,256]{2,0,1:T(8,128)S(1)}, u32[]{:S(2)}) copy-start(f32[32,7,256]{2,0,1:T(8,128)S(1)} %get-tuple-element.34) | copy-start | bytes 688132
  27.9 2.6 copy-start.29
  27.9 2.6 copy-start.30
  31.7 1.8 copy-start.5
  31.7 1.8 copy-start.22
  31.7 1.8 copy-start.31
  31.7 1.8 copy-start.33
  31.7 1.8 copy-start.35
  31.7 1.8 copy-start.37
  42.3 5.2 %copy-start.10 = (f32[32,7,256]{2,0,1:T(8,128)}, f32[32,7,256]{2,0,1:T(8,128)S(1)}, u32[]{:S(2)}) copy-start(f32[32,7,256]{2,0,1:T(8,128)S(1)} %get-tuple-element.29) | copy-start | bytes 688132
  42.3 5.2 %copy-start.12 = (f32[32,7,256]{2,0,1:T(8,128)}, f32[32,7,256]{2,0,1:T(8,128)S(1)}, u32[]{:S(2)}) copy-start(f32[32,7,256]{2,0,1:T(8,128)S(1)} %get-tuple-element.30) | copy-start | bytes 688132
  42.4 5.2 %copy-start.25 = (f32[32,1,256]{2,0,1:T(8,128)}, f32[32,1,256]{2,0,1:T(8,128)S(1)}, u32[]{:S(2)}) copy-start(f32[32,1,256]{2,0,1:T(8,128)S(1)} %get-tuple-element.31) | copy-start | bytes 98308
  42.4 5.2 %copy-start.27 = (f32[32,1,256]{2,0,1:T(8,128)}, f32[32,1,256]{2,0,1:T(8,128)S(1)}, u32[]{:S(2)}) copy-start(f32[32,1,256]{2,0,1:T(8,128)S(1)} %get-tuple-element.32) | copy-start | bytes 98308
  46.4 1.6 copy-start.24
  54.0 6.8 %copy-start.1 = (f32[32,8,16,16]{0,3,2,1:T(8,128)S(1)}, f32[32,8,16,16]{0,3,2,1:T(8,128)}, u32[]{:S(2)}) copy-start(f32[32,8,16,16]{0,3,2,1:T(8,128)} %get-tuple-element.11) | copy-start | bytes 786436
  61.9 2.1 copy-start.2
  61.9 2.4 copy-start.18
  61.9 2.4 copy-start.20
  61.9 2.4 copy-start.26
  61.9 2.4 copy-start.28
  95.9 86.5 %all-gather.4.cloned.1.call-start = ((), (), s32[]{:S(2)}) async-start(), calls=%async_computation.3 | async-start | bytes 3145728 | tf_op jit(solution)/shard_map/all_gather | solution.py:134
  96.7 188.6 %reduce-scatter.4.cloned.1.call-start = ((), (), s32[]{:S(2)}) async-start(), calls=%async_computation.5 | async-start | bytes 1114112
  (16 other events, 20.8 us)
Sparse Core Ops, SparseCore 0:
  96.0 67.0 all-gather.5
  165.0 17.4 all-gather.3
  207.3 77.8 reduce-scatter.3

commit v2 on v0

v2 whole, which is shorter than its diff:
```python
import functools

import jax
import jax.numpy as jnp
from jax import lax
from jax.experimental import pallas as pl
from jax.experimental.pallas import tpu as pltpu
from jax.sharding import Mesh
from jax.sharding import PartitionSpec as P

NXY = 16
SUBSTEPS = 3
HALO = SUBSTEPS

courant = 0.3
time_step = 0.5

SPACE = ("sx", "sy")
MODE = ("mz", "mc")


def neighbours(field):
    rows, planes, cells = field.shape
    grid = field.reshape(rows, planes, NXY, NXY)
    padded = jnp.pad(grid, ((0, 0), (0, 0), (1, 1), (1, 1)))
    lower_x = padded[:, :, :-2, 1:-1].reshape(field.shape)
    upper_x = padded[:, :, 2:, 1:-1].reshape(field.shape)
    lower_y = padded[:, :, 1:-1, :-2].reshape(field.shape)
    upper_y = padded[:, :, 1:-1, 2:].reshape(field.shape)
    return (lower_x, upper_x, lower_y, upper_y)


def upwind(field, below, above, velocity):
    lower_x, upper_x, lower_y, upper_y = neighbours(field)
    lowers = [lower_x, lower_y, below]
    uppers = [upper_x, upper_y, above]
    flux = jnp.zeros_like(field)
    for direction in range(3):
        speed = velocity[direction][:, None, None]
        flux = flux + jnp.maximum(speed, 0.0) * (field - lowers[direction])
        flux = flux + jnp.minimum(speed, 0.0) * (uppers[direction] - field)
    return field - courant * flux


def with_halo(block, sides, width):
    for axis, dim in sides:
        count = lax.axis_size(axis)
        forward = [(i, i + 1) for i in range(count - 1)]
        backward = [(target, source) for source, target in forward]
        low = lax.ppermute(
            lax.slice_in_dim(block, block.shape[dim] - width, None, axis=dim), axis, forward
        )
        high = lax.ppermute(lax.slice_in_dim(block, 0, width, axis=dim), axis, backward)
        block = jnp.concatenate([low, block, high], axis=dim)
    return block


def gain_kernel(t_ref, x_ref, xi_ref, o_ref, *, group, rows):
    z, _, jz, tile = x_ref.shape
    x = x_ref[...].reshape(z * jz, tile)
    xi = xi_ref[0].astype(jnp.float32)
    n_groups = o_ref.shape[1] // group

    def body(g, carry):
        start = pl.multiple_of(g * group * rows, group * rows)
        t = t_ref[pl.ds(start, group * rows), :]
        inner = jnp.dot(t, x, preferred_element_type=jnp.float32)
        inner = inner.reshape(group, rows, tile)
        o_ref[0, pl.ds(pl.multiple_of(g * group, group), group), :] = jnp.sum(
            inner * xi[None], axis=1
        )
        return carry

    lax.fori_loop(0, n_groups, body, 0)


def contract(tensor2d, gathered, factor, k_count, group=8):
    kr, width = tensor2d.shape
    rows = kr // k_count
    z, slabs, jz, tile = gathered.shape
    kernel = functools.partial(gain_kernel, group=group, rows=rows)
    cells = slabs * tile
    return pl.pallas_call(
        kernel,
        out_shape=jax.ShapeDtypeStruct((slabs, k_count, tile), jnp.float32),
        grid=(slabs,),
        in_specs=[
            pl.BlockSpec((kr, width), lambda c: (0, 0)),
            pl.BlockSpec((z, 1, jz, tile), lambda c: (0, c, 0, 0)),
            pl.BlockSpec((1, rows, tile), lambda c: (c, 0, 0)),
        ],
        out_specs=pl.BlockSpec((1, k_count, tile), lambda c: (c, 0, 0)),
        compiler_params=pltpu.CompilerParams(vmem_limit_bytes=48 * 1024 * 1024),
        cost_estimate=pl.CostEstimate(
            flops=2 * kr * width * cells + 2 * kr * cells,
            bytes_accessed=kr * width * 2 + width * cells * 2 + rows * cells * 2 + k_count * cells * 4,
            transcendentals=0,
        ),
    )(tensor2d, gathered, factor)


def swap_pair(x):
    return lax.ppermute(x, "mc", [(0, 1), (1, 0)])


def in_core_order(first_core, mine, other, axis):
    a = jnp.concatenate([mine, other], axis=axis)
    b = jnp.concatenate([other, mine], axis=axis)
    return jnp.where(first_core, a, b)


def per_device(density, tensor, velocity, inflow, flags):
    rows, depth, cells = density.shape
    position = lax.axis_index(SPACE)
    final = lax.axis_size(SPACE) - 1
    ghost_low = flags[0].astype(jnp.float32)[None, :] * inflow[:, None]
    ghost_high = flags[1].astype(jnp.float32)[None, :] * inflow[:, None]
    core = lax.axis_index("mc")
    first_core = core == 0

    other_tensor = swap_pair(tensor)

    field = density
    for substep in range(SUBSTEPS):
        padded = with_halo(field, ((SPACE, 1),), 1)
        low_plane = jnp.where(position == 0, ghost_low, padded[:, 0])
        high_plane = jnp.where(position == final, ghost_high, padded[:, -1])
        below = jnp.concatenate([low_plane[:, None], padded[:, 1:-2]], axis=1)
        above = jnp.concatenate([padded[:, 2:-1], high_plane[:, None]], axis=1)
        field = upwind(field, below, above, velocity)

    coarse = field.astype(jnp.bfloat16)
    keep = jnp.where(first_core, coarse[:, 0], coarse[:, 1])
    send = jnp.where(first_core, coarse[:, 1], coarse[:, 0])
    mine = in_core_order(first_core, keep, swap_pair(send), 0)
    modes = mine.shape[0]
    gathered = lax.all_gather(mine, ("mz", "sx", "sy"), axis=0, tiled=False)
    z_count = lax.axis_size("mz")
    count = lax.axis_size(SPACE)
    gathered = gathered.reshape(z_count, count, modes, cells)

    k_own, i_count, width = tensor.shape
    pair_tensor = in_core_order(first_core, tensor, other_tensor, 0)
    k_count = 2 * k_own
    start = position * i_count
    factor = lax.dynamic_slice(
        gathered, (start // modes, 0, start % modes, 0), (1, count, i_count, cells)
    ).reshape(count, i_count, cells)
    partial = contract(pair_tensor.reshape(k_count * i_count, width), gathered, factor, k_count)

    slabs = partial.shape[0]
    gain = lax.psum_scatter(
        partial.reshape(slabs * k_count, cells), SPACE, scatter_dimension=0, tiled=True
    )
    own_k = jnp.where(first_core, gain[:k_own], gain[k_own:])
    other_k = jnp.where(first_core, gain[k_own:], gain[:k_own])
    gain = in_core_order(first_core, own_k[:, None], swap_pair(other_k)[:, None], 1)
    return field + time_step * gain


def solution(mesh):
    devices = mesh.devices
    space, mode = devices.shape
    fine = Mesh(devices.reshape(4, space // 4, mode // 2, 2), SPACE + MODE)
    in_specs = (P(MODE, SPACE, None), P(MODE, SPACE, None), P(None, MODE), P(MODE), P())
    out_specs = P(MODE, SPACE, None)
    return jax.shard_map(
        per_device, mesh=fine, in_specs=in_specs, out_specs=out_specs, check_vma=False
    )
```

time: 197 us -> 286 us (1.45)
  waiting for transfers between devices: 73.8 us -> 203 us
  Pallas kernels: 0 us -> 33.5 us
  local copies, waits for them, and re-layouts: 37.3 us -> 5.44 us
  blocking collectives: 24.7 us -> 0 us
  matrix products: 23.2 us -> 0 us
  starting transfers between devices: 16.2 us -> 24.2 us
    reduce_scatter x0 -> x1, waiting for transfers between devices: none -> 78.2 us  [per_device(): lax.psum_scatter(partial.reshape(slabs * k_count, cells), SPACE, scatter_...]
    all_gather x1, waiting for transfers between devices: 67.3 us -> 115 us  [per_device(): gathered = lax.all_gather(mine, ('mz', 'sx', 'sy'), axis=0, tiled=False)]
    pallas_call x0 -> x1, Pallas kernels: none -> 33.5 us  [contract(): pl.pallas_call(kernel, out_shape=jax.ShapeDtypeStruct((slabs, k_count, ti...]
    unnamed x5 -> x9, local copies, waits for them, and re-layouts: 33.6 us -> 0.98 us
    all_gather x1 -> x0, blocking collectives: 24.7 us -> none  [per_device(): full_modes = lax.all_gather(coarse, 'mode', axis=0, tiled=True)]
    dot_general x1 -> x0, matrix products: 23.2 us -> none  [per_device(): jnp.dot(piece.reshape(out_rows * count, width), columns, preferred_elemen...]
    ppermute x0 -> x3, starting transfers between devices: none -> 7.28 us  [swap_pair(): return lax.ppermute(x, 'mc', [(0, 1), (1, 0)])]
    ppermute x0 -> x3, waiting for transfers between devices: none -> 4.15 us  [swap_pair(): return lax.ppermute(x, 'mc', [(0, 1), (1, 0)])]
  transfers between devices with their start and end apart: 7 -> 11, of which waited for: 3 -> 7; matrix products, arithmetic and copies ran while one was open for 5% -> 2% of each run, Pallas kernels for 0% -> 0%
where the time goes in v2:
time: 286 us; the launch traced here: 285 us
  waiting for transfers between devices  203 us (71%)
  Pallas kernels  33.5 us (12%)
  starting transfers between devices  24.2 us (8%)
  between operations  13.6 us (5%)
  local copies, waits for them, and re-layouts  5.44 us (2%)
  other arithmetic  5.43 us (2%)
    all_gather x1, waiting for transfers between devices, per_device(): gathered = lax.all_gather(mine, ('mz', 'sx', 'sy'), axis=0, tiled=False)  115 us
    reduce_scatter x1, waiting for transfers between devices, per_device(): lax.psum_scatter(partial.reshape(slabs * k_count, cells), SPACE, scatter_...  78.2 us
    pallas_call x1, Pallas kernels, contract(): pl.pallas_call(kernel, out_shape=jax.ShapeDtypeStruct((slabs, k_count, ti...  33.5 us
    ppermute x3, starting transfers between devices, with_halo(): lax.ppermute(lax.slice_in_dim(block, block.shape[dim] - width, None, axis...  13 us
    ppermute x3, starting transfers between devices, swap_pair(): return lax.ppermute(x, 'mc', [(0, 1), (1, 0)])  7.28 us
    ppermute x3, waiting for transfers between devices, with_halo(): lax.ppermute(lax.slice_in_dim(block, 0, width, axis=dim), axis, backward)  6 us
  transfers between devices with their start and end apart: 11, of which 7 were waited for; matrix products, arithmetic and copies ran while one was open for 2% of the time, Pallas kernels for 0%

profile of v2, /device:TPU:1, one launch (start us, length us, event | category | flops | bytes accessed | tf_op | source)
XLA Modules:
  0.0 285.2 jit_solution(1351622612440720188)
XLA Ops:
  6.5 1.0 fusion.24
  7.6 1.3 collective-permute-start.1
  8.9 4.6 %collective-permute-start = (f32[32,1,256]{2,0,1:T(8,128)S(1)}, f32[32,1,256]{2,0,1:T(8,128)S(1)}, u32[]{:S(2)}, u32[]{:S(2)}) collective-permute-start(f32[32,1,256]{2,0,1:T(8,128)S(1)} %copy.105), channel_id=1, source_target_pairs={{0,16},{16,32},{32,48},{48,64},{64,80},{80,96},{96,112},{112,128},... | collective-permute-start | bytes 98312 | tf_op jit(solution)/shard_map/ppermute | solution.py:50
  13.6 1.0 copy.78
  14.5 0.8 slice_convert_fusion
  15.3 0.8 maximum_bitcast_fusion.2
  16.9 0.1 copy.92
  17.0 3.4 %collective-permute-start.2 = (f32[32,1,256]{2,0,1:T(8,128)S(1)}, f32[32,1,256]{2,0,1:T(8,128)S(1)}, u32[]{:S(2)}, u32[]{:S(2)}) collective-permute-start(f32[32,1,256]{2,0,1:T(8,128)S(1)} %get-tuple-element.23), channel_id=1, source_target_pairs={{0,16},{16,32},{32,48},{48,64},{64,80},{80,96},{96,112},{112,128},... | collective-permute-start | bytes 98312 | tf_op jit(solution)/shard_map/ppermute | solution.py:50
  20.4 1.3 collective-permute-start.3
  21.8 0.1 copy.94
  21.9 0.1 copy.95
  22.1 0.1 copy.96
  22.2 2.8 collective-permute-done.3
  25.2 0.1 copy.97
  25.4 5.0 %collective-permute-start.4 = (f32[32,1,256]{2,0,1:T(8,128)S(1)}, f32[32,1,256]{2,0,1:T(8,128)S(1)}, u32[]{:S(2)}, u32[]{:S(2)}) collective-permute-start(f32[32,1,256]{2,0,1:T(8,128)S(1)} %get-tuple-element.21), channel_id=1, source_target_pairs={{0,16},{16,32},{32,48},{48,64},{64,80},{80,96},{96,112},{112,128},... | collective-permute-start | bytes 98312 | tf_op jit(solution)/shard_map/ppermute | solution.py:50
  30.4 1.3 collective-permute-start.5
  32.2 3.2 %collective-permute-done.5 = f32[32,1,256]{2,0,1:T(8,128)S(1)} collective-permute-done((f32[32,1,256]{2,0,1:T(8,128)S(1)}, f32[32,1,256]{2,0,1:T(8,128)S(1)}, u32[]{:S(2)}, u32[]{:S(2)}) %collective-permute-start.5) | collective-permute-done | bytes 32800 | tf_op jit(solution)/shard_map/ppermute | solution.py:53
  35.4 0.1 fusion.20
  35.5 4.5 %collective-permute-start.7 = (bf16[32,256]{1,0:T(8,128)(2,1)S(1)}, bf16[32,256]{1,0:T(8,128)(2,1)S(1)}, u32[]{:S(2)}, u32[]{:S(2)}) collective-permute-start(bf16[32,256]{1,0:T(8,128)(2,1)S(1)} %get-tuple-element.28), channel_id=1, source_target_pairs={{0,1},{1,0},{2,3},{3,2},{4,5},{5,4},{6,7},{7,6},{8,9},{9,8},{10,11... | collective-permute-start | bytes 49160 | tf_op jit(solution)/shard_map/ppermute | solution.py:103
  40.0 0.8 collective-permute-done.7
  40.9 0.6 maximum_select_fusion.2
  41.6 0.4 collective-permute-start.6
  42.0 2.4 collective-permute-done.6
  44.5 1.9 maximum_select_fusion
  46.3 114.7 %all-gather.2.cloned.1.call-done = bf16[128,64,256]{2,1,0:T(8,128)(2,1)} async-done(((bf16[1,64,256]{2,1,0:T(8,128)(2,1)}), bf16[128,64,256]{2,1,0:T(8,128)(2,1)}) %all-gather.2.cloned.1.call-update) | async-done | bytes 4194320 | tf_op jit(solution)/shard_map/all_gather | solution.py:137
  161.0 1.0 dynamic-slice_bitcast_fusion.xi_ref
  162.0 33.5 %shard_map.55 = f32[16,64,256]{2,1,0:T(8,128)} custom-call(bf16[2048,512]{1,0:T(8,128)(2,1)S(1)} %bitcast.42, bf16[8,16,64,256]{3,2,1,0:T(8,128)(2,1)} %bitcast.66, bf16[16,32,256]{2,1,0:T(8,128)(2,1)S(1)} %dynamic-slice_bitcast_fusion.xi_ref), custom_call_target="tpu_custom_call" | custom-call | flops 8606711808 | bytes 7602176 | tf_op jit(solution)/shard_map/pallas_call | solution.py:83
  195.5 78.2 %reduce-scatter.2.cloned.1.call-done = f32[64,256]{1,0:T(8,128)} async-done(((f32[1024,256]{1,0:T(8,128)}), f32[64,256]{1,0:T(8,128)}) %reduce-scatter.2.cloned.1.call-update) | async-done | bytes 65552 | tf_op jit(solution)/shard_map/reduce_scatter | solution.py:152
  273.6 0.8 select_bitcast_fusion
  274.4 2.4 collective-permute-start.8
  276.8 0.9 collective-permute-done.8
  277.7 0.7 copy.102
  (37 shorter events, 1.8 us)
Async XLA Ops:
  6.5 10.2 %copy-start.1 = (f32[32,2,256]{2,1,0:T(2,128)S(1)}, f32[32,2,256]{2,1,0:T(2,128)}, u32[]{:S(2)}) copy-start(f32[32,2,256]{2,1,0:T(2,128)} %param.5) | copy-start | bytes 196612
  6.5 10.1 %copy-start.2 = (f32[32]{0:T(128)S(1)}, f32[32]{0:T(128)}, u32[]{:S(2)}) copy-start(f32[32]{0:T(128)} %param.8) | copy-start | bytes 388
  6.5 154.5 %all-gather.2.cloned.1.call-start = ((), (), s32[]{:S(2)}) async-start(), calls=%async_computation.1 | async-start | bytes 4227072 | tf_op jit(solution)/shard_map/all_gather | solution.py:137
  7.6 9.0 %collective-permute-start.1 = (f32[32,1,256]{2,0,1:T(8,128)S(1)}, f32[32,1,256]{2,0,1:T(8,128)S(1)}, u32[]{:S(2)}, u32[]{:S(2)}) collective-permute-start(f32[32,1,256]{2,0,1:T(8,128)S(1)} %copy.104), channel_id=1, source_target_pairs={{16,0},{32,16},{48,32},{64,48},{80,64},{96,80},{112,96},{128,112},... | collective-permute-start | bytes 98312 | tf_op jit(solution)/shard_map/ppermute | solution.py:53
  8.9 7.7 %collective-permute-start = (f32[32,1,256]{2,0,1:T(8,128)S(1)}, f32[32,1,256]{2,0,1:T(8,128)S(1)}, u32[]{:S(2)}, u32[]{:S(2)}) collective-permute-start(f32[32,1,256]{2,0,1:T(8,128)S(1)} %copy.105), channel_id=1, source_target_pairs={{0,16},{16,32},{32,48},{48,64},{64,80},{80,96},{96,112},{112,128},... | collective-permute-start | bytes 98312 | tf_op jit(solution)/shard_map/ppermute | solution.py:50
  17.0 5.2 %collective-permute-start.2 = (f32[32,1,256]{2,0,1:T(8,128)S(1)}, f32[32,1,256]{2,0,1:T(8,128)S(1)}, u32[]{:S(2)}, u32[]{:S(2)}) collective-permute-start(f32[32,1,256]{2,0,1:T(8,128)S(1)} %get-tuple-element.23), channel_id=1, source_target_pairs={{0,16},{16,32},{32,48},{48,64},{64,80},{80,96},{96,112},{112,128},... | collective-permute-start | bytes 98312 | tf_op jit(solution)/shard_map/ppermute | solution.py:50
  20.4 4.7 %collective-permute-start.3 = (f32[32,1,256]{2,0,1:T(8,128)S(1)}, f32[32,1,256]{2,0,1:T(8,128)S(1)}, u32[]{:S(2)}, u32[]{:S(2)}) collective-permute-start(f32[32,1,256]{2,0,1:T(8,128)S(1)} %get-tuple-element.24), channel_id=1, source_target_pairs={{16,0},{32,16},{48,32},{64,48},{80,64},{96,80},{112,96},{128,112},... | collective-permute-start | bytes 98312 | tf_op jit(solution)/shard_map/ppermute | solution.py:53
  25.2 16.4 %copy-start = (bf16[32,32,512]{2,1,0:T(8,128)(2,1)S(1)}, bf16[32,32,512]{2,1,0:T(8,128)(2,1)}, u32[]{:S(2)}) copy-start(bf16[32,32,512]{2,1,0:T(8,128)(2,1)} %param.6) | copy-start | bytes 3145732
  25.4 6.8 %collective-permute-start.4 = (f32[32,1,256]{2,0,1:T(8,128)S(1)}, f32[32,1,256]{2,0,1:T(8,128)S(1)}, u32[]{:S(2)}, u32[]{:S(2)}) collective-permute-start(f32[32,1,256]{2,0,1:T(8,128)S(1)} %get-tuple-element.21), channel_id=1, source_target_pairs={{0,16},{16,32},{32,48},{48,64},{64,80},{80,96},{96,112},{112,128},... | collective-permute-start | bytes 98312 | tf_op jit(solution)/shard_map/ppermute | solution.py:50
  30.4 5.0 %collective-permute-start.5 = (f32[32,1,256]{2,0,1:T(8,128)S(1)}, f32[32,1,256]{2,0,1:T(8,128)S(1)}, u32[]{:S(2)}, u32[]{:S(2)}) collective-permute-start(f32[32,1,256]{2,0,1:T(8,128)S(1)} %get-tuple-element.22), channel_id=1, source_target_pairs={{16,0},{32,16},{48,32},{64,48},{80,64},{96,80},{112,96},{128,112},... | collective-permute-start | bytes 98312 | tf_op jit(solution)/shard_map/ppermute | solution.py:53
  35.5 5.3 %collective-permute-start.7 = (bf16[32,256]{1,0:T(8,128)(2,1)S(1)}, bf16[32,256]{1,0:T(8,128)(2,1)S(1)}, u32[]{:S(2)}, u32[]{:S(2)}) collective-permute-start(bf16[32,256]{1,0:T(8,128)(2,1)S(1)} %get-tuple-element.28), channel_id=1, source_target_pairs={{0,1},{1,0},{2,3},{3,2},{4,5},{5,4},{6,7},{7,6},{8,9},{9,8},{10,11... | collective-permute-start | bytes 49160 | tf_op jit(solution)/shard_map/ppermute | solution.py:103
  41.5 232.1 %reduce-scatter.2.cloned.1.call-start = ((), (), s32[]{:S(2)}) async-start(), calls=%async_computation.2 | async-start | bytes 1114112 | tf_op jit(solution)/shard_map/reduce_scatter | solution.py:152
  41.6 2.9 %collective-permute-start.6 = (bf16[32,32,512]{2,1,0:T(8,128)(2,1)S(1)}, bf16[32,32,512]{2,1,0:T(8,128)(2,1)}, u32[]{:S(2)}, u32[]{:S(2)}) collective-permute-start(bf16[32,32,512]{2,1,0:T(8,128)(2,1)S(1)} %copy-done), channel_id=1, source_target_pairs={{0,1},{1,0},{2,3},{3,2},{4,5},{5,4},{6,7},{7,6},{8,9},{9,8},{10,11... | collective-permute-start | bytes 3145736 | tf_op jit(solution)/shard_map/ppermute | solution.py:103
  274.4 3.2 %collective-permute-start.8 = (f32[32,256]{1,0:T(8,128)S(1)}, f32[32,256]{1,0:T(8,128)S(1)}, u32[]{:S(2)}, u32[]{:S(2)}) collective-permute-start(f32[32,256]{1,0:T(8,128)S(1)} %get-tuple-element.20), channel_id=1, source_target_pairs={{0,1},{1,0},{2,3},{3,2},{4,5},{5,4},{6,7},{7,6},{8,9},{9,8},{10,11... | collective-permute-start | bytes 98312 | tf_op jit(solution)/shard_map/ppermute | solution.py:103
Sparse Core Ops, SparseCore 0:
  41.6 119.3 all-gather.1
  195.6 77.9 reduce-scatter.1
